TPU v7x, 256 devices: a whole 4x4x8 slice. The times are simulated.
256 devices in a mesh: ctx: 16 (over x, y), tp: 16 (over z, core).
Axes of the slice: x: 4, y: 4, z: 8, core: 2. Of those that a mesh axis runs over, the one named last changes fastest.
Arguments:
- tokens: bfloat16 [16384, 2560], P(('ctx', 'tp')), may hold values from -8 to 8
- norm1_gain: float32 [2560], replicated, may hold values from 0.1 to 1.9
- w_z: bfloat16 [2560, 5120], P(None, 'tp'), may hold values from -0.125 to 0.125
- w_x: bfloat16 [2560, 5120], P(None, 'tp'), may hold values from -0.125 to 0.125
- w_bc: bfloat16 [2560, 256], replicated, may hold values from -0.125 to 0.125
- w_dt: bfloat16 [2560, 80], P(None, 'tp'), may hold values from -1 to 1
- dt_bias: float32 [80], P('tp'), may hold values from -5.5 to -4
- a_log: float32 [80], P('tp'), may hold values from -12 to 1.4
- conv_x: float32 [4, 5120], P(None, 'tp'), may hold values from -3 to 3
- conv_bc: float32 [4, 256], replicated, may hold values from -3 to 3
- d_skip: float32 [80], P('tp'), may hold values from 0.1 to 1.9
- ssm_gain: float32 [5120], P('tp'), may hold values from 0.1 to 1.9
- w_out: bfloat16 [5120, 2560], P('tp'), may hold values from -0.078125 to 0.078125
- norm2_gain: float32 [2560], replicated, may hold values from 0.1 to 1.9
- w_gate: bfloat16 [2560, 5120], P(None, 'tp'), may hold values from -0.125 to 0.125
- w_up: bfloat16 [2560, 5120], P(None, 'tp'), may hold values from -0.125 to 0.125
- w_down: bfloat16 [5120, 2560], P('tp'), may hold values from -0.078125 to 0.078125
Outputs:
- layer_out: bfloat16 [16384, 2560], P(('ctx', 'tp'))
All inputs are finite; a program needn't handle non-finite values.
Results may differ from a plain program's by a relative error of at most 0.017.
Values may be sent and summed in bfloat16 or wider, within the bound.
No kernel may reach another device: no remote copies, remote signals or barrier semaphores. Data moves between devices by JAX's collectives and lax.ppermute only.
A program may use at most 128 MiB of HBM per device.

v0:
```python
import jax
import jax.numpy as jnp
from jax import lax
from jax.sharding import PartitionSpec as P

HEADS = 80
HEAD_DIM = 64
STATE_DIM = 128
BLOCK_LEN = 256
EPS = 1e-05


def from_behind(value, axis, steps):
    count = lax.axis_size(axis)
    first, last = (max(0, -steps), min(count, count - steps))
    return lax.ppermute(value, axis, [(source, source + steps) for source in range(first, last)])


def carried_in(shard, axis, join, neutral):
    place = lax.axis_index(axis)
    gathered = jax.tree.map(
        lambda a, kind: lax.all_gather(a.astype(kind), axis), shard, (jnp.bfloat16, jnp.bfloat16)
    )
    state = jax.tree.map(lambda a, e: jnp.zeros_like(a) + jnp.asarray(e, a.dtype), shard, neutral)

    def one(step, state):
        return join(
            state,
            jax.tree.map(
                lambda a, own: lax.dynamic_index_in_dim(a, step, 0, False).astype(own.dtype),
                gathered,
                shard,
            ),
        )

    return lax.fori_loop(0, place, one, state)


def rms_rows(values, gain):
    wide = values.astype(jnp.float32)
    return wide * lax.rsqrt(jnp.mean(wide * wide, axis=-1, keepdims=True) + EPS) * gain


def conv_four(rim, current, kernel):
    extended = jnp.concatenate([rim, current], axis=0).astype(jnp.float32)
    length = current.shape[0]
    result = kernel[0] * extended[0:length]
    for offset in range(1, 4):
        result = result + kernel[offset] * extended[offset : offset + length]
    return result


def combine_states(prior_part, next_part):
    return (
        prior_part[0] * next_part[0],
        next_part[1] + next_part[0][:, None, None] * prior_part[1],
    )


def carry_step(state, pieces):
    decay_now, fresh = pieces
    return (decay_now[:, None, None] * state + fresh, state)


def local(
    tokens,
    norm1_gain,
    w_z,
    w_x,
    w_bc,
    w_dt,
    dt_bias,
    a_log,
    conv_x,
    conv_bc,
    d_skip,
    ssm_gain,
    w_out,
    norm2_gain,
    w_gate,
    w_up,
    w_down,
):
    gathered = lax.all_gather(tokens, "tp", axis=0, tiled=True)
    normed = rms_rows(gathered, norm1_gain).astype(jnp.bfloat16)
    bc_rows = jnp.dot(normed, w_bc, preferred_element_type=jnp.float32).astype(jnp.bfloat16)
    group_len = gathered.shape[0]
    head_count = w_dt.shape[1]
    channels = w_x.shape[1]
    gate_z = jnp.dot(normed, w_z, preferred_element_type=jnp.float32)
    inner_rows = jnp.dot(normed, w_x, preferred_element_type=jnp.float32).astype(jnp.bfloat16)
    dt_raw = jnp.dot(normed, w_dt, preferred_element_type=jnp.float32)
    rim_inner, rim_bc = from_behind((inner_rows[-3:], bc_rows[-3:]), "ctx", 1)
    conv_inner = jax.nn.silu(conv_four(rim_inner, inner_rows, conv_x)).astype(jnp.bfloat16)
    conv_bcm = jax.nn.silu(conv_four(rim_bc, bc_rows, conv_bc)).astype(jnp.bfloat16)
    dt_step = jax.nn.softplus(dt_raw + dt_bias)
    log_decay = -dt_step * jnp.exp(a_log)
    block_count = group_len // BLOCK_LEN
    log_blocks = log_decay.reshape(block_count, BLOCK_LEN, head_count)
    step_blocks = dt_step.reshape(block_count, BLOCK_LEN, head_count)
    cum_decay = jnp.cumsum(log_blocks, axis=1)
    b_mat = conv_bcm[:, :STATE_DIM].reshape(block_count, BLOCK_LEN, STATE_DIM)
    c_mat = conv_bcm[:, STATE_DIM:].reshape(block_count, BLOCK_LEN, STATE_DIM)
    scores = jnp.einsum("btn,bsn->bts", c_mat, b_mat, preferred_element_type=jnp.float32)
    causal_mask = jnp.tril(jnp.ones((BLOCK_LEN, BLOCK_LEN), dtype=bool))[None, :, :, None]
    decay_diff = jnp.where(causal_mask, cum_decay[:, :, None, :] - cum_decay[:, None, :, :], 0.0)
    weights = jnp.where(causal_mask, jnp.exp(decay_diff), 0.0)
    inner_wide = conv_inner.astype(jnp.float32).reshape(
        block_count, BLOCK_LEN, head_count, HEAD_DIM
    )
    scaled = inner_wide * step_blocks[..., None]
    mixed_w = scores[..., None] * weights
    y_intra = jnp.einsum("btsh,bshp->bthp", mixed_w, scaled, precision=lax.Precision.HIGHEST)
    block_last = cum_decay[:, -1, :]
    tail_decay = jnp.exp(block_last[:, None, :] - cum_decay)
    b_wide = b_mat.astype(jnp.float32)
    c_wide = c_mat.astype(jnp.float32)
    block_states = jnp.einsum(
        "bsh,bshp,bsn->bhpn", tail_decay, scaled, b_wide, precision=lax.Precision.HIGHEST
    )
    block_decay = jnp.exp(block_last)
    zero_state = jnp.zeros((head_count, HEAD_DIM, STATE_DIM), jnp.float32)
    local_final, local_in = lax.scan(carry_step, zero_state, (block_decay, block_states))
    total_decay = jnp.prod(block_decay, axis=0)
    prior_decay = jnp.exp(jnp.cumsum(block_last, axis=0) - block_last)
    identity = (jnp.ones((head_count,), jnp.float32), zero_state)
    incoming_decay, incoming = carried_in(
        (total_decay, local_final), "ctx", combine_states, identity
    )
    state_in = local_in + prior_decay[:, :, None, None] * incoming[None]
    y_inter = jnp.exp(cum_decay)[..., None] * jnp.einsum(
        "btn,bhpn->bthp", c_wide, state_in, precision=lax.Precision.HIGHEST
    )
    ssm_out = y_intra + y_inter + d_skip[None, None, :, None] * inner_wide
    gated = ssm_out.reshape(group_len, channels) * jax.nn.silu(gate_z)
    squares = lax.psum(jnp.sum(gated * gated, axis=-1), "tp")
    scaled_out = (gated * lax.rsqrt(squares / (HEADS * HEAD_DIM) + EPS)[:, None] * ssm_gain).astype(
        jnp.bfloat16
    )
    piece = scaled_out
    mixer_own = lax.psum_scatter(
        jnp.dot(piece, w_out, preferred_element_type=jnp.float32).astype(jnp.bfloat16),
        "tp",
        scatter_dimension=0,
        tiled=True,
    ).astype(jnp.float32)
    resid = (tokens.astype(jnp.float32) + mixer_own).astype(jnp.bfloat16)
    normed_own = rms_rows(resid, norm2_gain).astype(jnp.bfloat16)
    mlp_in = lax.all_gather(normed_own, "tp", axis=0, tiled=True)
    mlp_gate = jnp.dot(mlp_in, w_gate, preferred_element_type=jnp.float32)
    mlp_up = jnp.dot(mlp_in, w_up, preferred_element_type=jnp.float32)
    hidden = (jax.nn.silu(mlp_gate) * mlp_up).astype(jnp.bfloat16)
    piece = hidden
    mlp_down = lax.psum_scatter(
        jnp.dot(piece, w_down, preferred_element_type=jnp.float32).astype(jnp.bfloat16),
        "tp",
        scatter_dimension=0,
        tiled=True,
    ).astype(jnp.float32)
    return (resid.astype(jnp.float32) + mlp_down).astype(jnp.bfloat16)


def solution(mesh):
    return jax.shard_map(
        local,
        mesh=mesh,
        in_specs=(
            P(("ctx", "tp"), None),
            P(),
            P(None, "tp"),
            P(None, "tp"),
            P(),
            P(None, "tp"),
            P("tp"),
            P("tp"),
            P(None, "tp"),
            P(),
            P("tp"),
            P("tp"),
            P("tp", None),
            P(),
            P(None, "tp"),
            P(None, "tp"),
            P("tp", None),
        ),
        out_specs=P(("ctx", "tp"), None),
        check_vma=False,
    )
```

profile of v0, /device:TPU:4, one launch (start us, length us, event | category | flops | bytes accessed | tf_op | source)
XLA Modules:
  0.0 396.0 jit_solution(1112012405852655867)
XLA Ops:
  9.7 45.6 %all-gather.6.cloned.1.call-done = bf16[1024,2560]{1,0:T(8,128)(2,1)} async-done(((bf16[64,2560]{1,0:T(8,128)(2,1)}), bf16[1024,2560]{1,0:T(8,128)(2,1)}) %all-gather.6.cloned.1.call-update) | async-done | bytes 5242896 | tf_op jit(solution)/shard_map/all_gather | solution.py:84
  55.3 3.7 fusion.1
  63.0 6.0 %reduce-window.6 = f32[4,5,2,128]{3,2,1,0:T(2,128)S(1)} reduce-window(f32[4,5,2,128]{3,2,1,0:T(2,128)S(1)} %copy.46, f32[]{:T(128)} %constant.61.clone.1), window={size=1x1x1x128 pad=0_0x0_0x0_0x127_0}, to_apply=%region_1.2 | reduce-window | flops 650240 | bytes 40964 | tf_op jit(solution)/shard_map/reduce-window
  70.0 4.5 %convolution_convert_fusion.3 = bf16[1024,256]{1,0:T(8,128)(2,1)S(1)} fusion(bf16[1024,2560]{1,0:T(8,128)(2,1)} %copy-done.1, bf16[2560,256]{1,0:T(8,128)(2,1)} %param.25), kind=kOutput, calls=%fused_computation.44 | convolution fusion | flops 1342439424 | bytes 7077888 | tf_op jit(solution)/shard_map/dot_general | solution.py:86
  74.5 3.4 collective-permute-start.1
  80.0 3.4 collective-permute-start
  84.2 4.2 %collective-permute-done = bf16[3,320]{0,1:T(8,128)(2,1)S(1)} collective-permute-done((bf16[3,320]{0,1:T(8,128)(2,1)S(1)}, bf16[3,320]{0,1:T(8,128)(2,1)S(1)}, u32[]{:S(2)}, u32[]{:S(2)}) %collective-permute-start) | collective-permute-done | bytes 1952 | tf_op jit(solution)/shard_map/ppermute | solution.py:16
  88.7 2.4 fusion.40
  91.2 2.8 reshape.107
  94.0 2.2 fusion.24
  96.2 3.2 while.26
  101.7 31.3 %all-reduce = bf16[80]{0:T(256)(128)(2,1)S(1)} all-reduce(bf16[80]{0:T(256)(128)(2,1)S(1)} %dynamic-update-slice), channel_id=3, replica_groups=mesh['ctx'=16,'tp'=16] {'ctx'}, use_global_device_ids=true, to_apply=%add | all-reduce | flops 80 | bytes 320
  133.4 8.5 %fusion.17 = f32[4,256,5,64]{1,3,2,0:T(8,128)} fusion(f32[4,256,5]{1,2,0:T(8,128)S(1)} %copy.50, f32[4,256,256]{2,1,0:T(8,128)S(1)} %fusion.50, pred[256,256]{1,0:T(8,128)(4,1)S(1)} %iota_compare_fusion, f32[4,256,5,64]{1,0,3,2:T(4,128)} %reshape.107, f32[4,256,5]{1,2,0:T(8,128)S(1)} %bitcast.98), kind=kOutput, calls=%fused_computation.28 | convolution fusion | flops 1012203520 | bytes 3776512 | tf_op jit(solution)/shard_map/btsh,bshp->bthp/dot_general | solution.py:113
  141.9 2.0 all-gather.10.cloned.1.call-done
  143.9 8.3 %while.25 = (s32[]{:T(128)}, f32[5,64,128]{2,1,0:T(8,128)S(1)}, s32[]{:T(128)}, bf16[16,5,64,128]{3,2,1,0:T(8,128)(2,1)}, bf16[16,5]{1,0:T(8,128)(2,1)S(1)}, /*index=5*/s32[]{:T(128)}, s32[]{:T(128)}, s32[]{:T(128)}) while((s32[]{:T(128)}, f32[5,64,128]{2,1,0:T(8,128)S(1)}, s32[]{:T(128)}, bf16[16,5,64,128]{3,2,1,0:T(8,128)(2,1)}, ...), condition=%wide.region_8.9_spmd, body=%wide.region_7.8_spmd.sunk | while | flops 122890 | bytes 409785 | solution.py:36
  152.2 3.0 fusion.16
  158.0 3.1 multiply_reduce_fusion
  161.1 23.9 %psum.7 = f32[1024]{0:T(1024)S(1)} all-reduce(f32[1024]{0:T(1024)S(1)} %get-tuple-element.135), channel_id=1, replica_groups=mesh['ctx'=16,'tp'=16] {'tp'}, use_global_device_ids=true, to_apply=%region_10.11 | all-reduce | flops 1024 | bytes 8192 | tf_op jit(solution)/shard_map/psum | solution.py:136
  185.1 6.8 %convolution_convert_fusion.1 = bf16[1024,2560]{1,0:T(8,128)(2,1)} fusion(bf16[320,2560]{1,0:T(8,128)(2,1)S(1)} %copy-done, f32[320]{0:T(512)S(1)} %copy-done.13, f32[1024]{0:T(1024)S(1)} %add_rsqrt_fusion, f32[1024,320]{0,1:T(8,128)} %bitcast.94, f32[1024,320]{0,1:T(8,128)} %get-tuple-element.136), kind=kOutput, calls=%fused_computation.12 | convolution fusion | flops 1682964480 | bytes 9508096 | tf_op jit(solution)/shard_map/dot_general | solution.py:142
  192.0 71.4 %reduce-scatter.3.cloned.1.call-done = bf16[64,2560]{1,0:T(8,128)(2,1)} async-done(((bf16[1024,2560]{1,0:T(8,128)(2,1)}), bf16[64,2560]{1,0:T(8,128)(2,1)}) %reduce-scatter.3.cloned.1.call-update) | async-done | bytes 327696 | tf_op jit(solution)/shard_map/reduce_scatter | solution.py:141
  266.7 41.6 %all-gather.8.cloned.1.call-done = bf16[1024,2560]{1,0:T(8,128)(2,1)} async-done(((bf16[64,2560]{1,0:T(8,128)(2,1)}), bf16[1024,2560]{1,0:T(8,128)(2,1)}) %all-gather.8.cloned.1.call-update) | async-done | bytes 5242896 | tf_op jit(solution)/shard_map/all_gather | solution.py:149
  308.3 4.9 %fusion.51 = f32[1024,320]{0,1:T(8,128)S(1)} fusion(bf16[1024,2560]{1,0:T(8,128)(2,1)} %all-gather.8.cloned.1.call-done, bf16[2560,320]{0,1:T(8,128)(2,1)} %param.35), kind=kOutput, calls=%fused_computation.98 | convolution fusion | flops 1677721600 | bytes 8192000 | tf_op jit(solution)/shard_map/dot_general | solution.py:150
  313.2 10.4 %convolution_convert_fusion = bf16[1024,2560]{1,0:T(8,128)(2,1)} fusion(bf16[320,2560]{1,0:T(8,128)(2,1)} %param.37, bf16[1024,2560]{1,0:T(8,128)(2,1)} %all-gather.8.cloned.1.call-done, bf16[2560,320]{0,1:T(8,128)(2,1)} %param.36, f32[1024,320]{0,1:T(8,128)S(1)} %fusion.51), kind=kOutput, calls=%fused_computation.11 | convolution fusion | flops 3360030720 | bytes 15073280 | tf_op jit(solution)/shard_map/dot_general | solution.py:155
  323.6 64.0 %reduce-scatter.5.cloned.1.call-done = bf16[64,2560]{1,0:T(8,128)(2,1)} async-done(((bf16[1024,2560]{1,0:T(8,128)(2,1)}), bf16[64,2560]{1,0:T(8,128)(2,1)}) %reduce-scatter.5.cloned.1.call-update) | async-done | bytes 327696 | tf_op jit(solution)/shard_map/reduce_scatter | solution.py:154
  (129 shorter events, 32.1 us)
Async XLA Ops:
  6.5 178.5 %copy-start = (bf16[320,2560]{1,0:T(8,128)(2,1)S(1)}, bf16[320,2560]{1,0:T(8,128)(2,1)}, u32[]{:S(2)}) copy-start(bf16[320,2560]{1,0:T(8,128)(2,1)} %param.33) | copy-start | bytes 4915204
  6.5 48.8 %all-gather.6.cloned.1.call-start = ((), (), s32[]{:S(2)}) async-start(), calls=%async_computation.2 | async-start | bytes 5570560 | tf_op jit(solution)/shard_map/all_gather | solution.py:84
  7.3 136.6 %all-gather.10.cloned.1.call-start = ((), (), s32[]{:S(2)}) async-start(), calls=%async_computation.6 | async-start | bytes 1392640 | tf_op jit(solution)/shard_map/all_gather | solution.py:22
  9.7 49.3 %copy-start.7 = (f32[2560]{0:T(1024)S(1)}, f32[2560]{0:T(1024)}, u32[]{:S(2)}) copy-start(f32[2560]{0:T(1024)} %param.22) | copy-start | bytes 30724
  55.3 4.0 %copy-start.2 = (bf16[1024,2560]{1,0:T(8,128)(2,1)S(1)}, bf16[1024,2560]{1,0:T(8,128)(2,1)}, u32[]{:S(2)}) copy-start(bf16[1024,2560]{1,0:T(8,128)(2,1)} %all-gather.6.cloned.1.call-done) | copy-start | bytes 15728644
  60.6 2.3 copy-start.1
  69.5 8.4 %slice-start = ((s8[5242880]{0:T(1024)(128)(4,1)}), s8[1048576]{0:T(1024)(128)(4,1)S(1)}, s32[]{:S(2)}) async-start(s8[5242880]{0:T(1024)(128)(4,1)} %bitcast.84), calls=%async_computation.7 | async-start | bytes 2097152
  70.0 8.0 %slice-start.1 = ((s8[5242880]{0:T(1024)(128)(4,1)}), s8[4194304]{0:T(1024)(128)(4,1)S(1)}, s32[]{:S(2)}) async-start(s8[5242880]{0:T(1024)(128)(4,1)} %bitcast.84), calls=%async_computation.8 | async-start | bytes 8388608
  70.0 8.0 %copy-start.11 = (bf16[2560,320]{0,1:T(8,128)(2,1)S(1)}, bf16[2560,320]{0,1:T(8,128)(2,1)}, u32[]{:S(2)}) copy-start(bf16[2560,320]{0,1:T(8,128)(2,1)} %param.24) | copy-start | bytes 4915204
  74.5 8.9 %collective-permute-start.1 = (bf16[3,256]{1,0:T(4,128)(2,1)S(1)}, bf16[3,256]{1,0:T(4,128)(2,1)S(1)}, u32[]{:S(2)}, u32[]{:S(2)}) collective-permute-start(bf16[3,256]{1,0:T(4,128)(2,1)S(1)} %slice.97), channel_id=1, source_target_pairs={{0,16},{16,32},{32,48},{48,64},{64,80},{80,96},{96,112},{112,128},... | collective-permute-start | bytes 4616 | tf_op jit(solution)/shard_map/ppermute | solution.py:16
  80.0 8.4 %collective-permute-start = (bf16[3,320]{0,1:T(8,128)(2,1)S(1)}, bf16[3,320]{0,1:T(8,128)(2,1)S(1)}, u32[]{:S(2)}, u32[]{:S(2)}) collective-permute-start(bf16[3,320]{0,1:T(8,128)(2,1)S(1)} %slice.92), channel_id=1, source_target_pairs={{0,16},{16,32},{32,48},{48,64},{64,80},{80,96},{96,112},{112,128},... | collective-permute-start | bytes 5768 | tf_op jit(solution)/shard_map/ppermute | solution.py:16
  96.1 4.0 %copy-start.14 = (u32[256]{0:T(256)S(1)}, u32[256]{0:T(256)}, u32[]{:S(2)}) copy-start(u32[256]{0:T(256)} %constant.76) | copy-start | bytes 3076
  100.0 163.3 %reduce-scatter.3.cloned.1.call-start = ((), (), s32[]{:S(2)}) async-start(), calls=%async_computation.3 | async-start | bytes 5570560 | tf_op jit(solution)/shard_map/reduce_scatter | solution.py:141
  141.9 10.3 %copy-start.10 = (f32[5]{0:T(128)S(1)}, f32[5]{0:T(128)}, u32[]{:S(2)}) copy-start(f32[5]{0:T(128)} %param.31) | copy-start | bytes 64
  143.9 12.5 %slice-start.2 = ((s8[5242880]{0:T(1024)(128)(4,1)}), s8[1048576]{0:T(1024)(128)(4,1)S(1)}, s32[]{:S(2)}) async-start(s8[5242880]{0:T(1024)(128)(4,1)} %bitcast.86), calls=%async_computation.9 | async-start | bytes 2097152
  152.2 4.2 %slice-start.3 = ((s8[5242880]{0:T(1024)(128)(4,1)}), s8[4194304]{0:T(1024)(128)(4,1)S(1)}, s32[]{:S(2)}) async-start(s8[5242880]{0:T(1024)(128)(4,1)} %bitcast.86), calls=%async_computation.10 | async-start | bytes 8388608
  156.1 1.9 copy-start.12
  156.4 4.7 %copy-start.5 = (f32[40,8,4,256]{3,1,2,0:T(8,128)}, f32[40,8,4,256]{3,1,2,0:T(8,128)S(1)}, u32[]{:S(2)}) copy-start(f32[40,8,4,256]{3,1,2,0:T(8,128)S(1)} %copy.60) | copy-start | bytes 3932164
  158.0 27.1 %copy-start.13 = (f32[320]{0:T(512)S(1)}, f32[320]{0:T(512)}, u32[]{:S(2)}) copy-start(f32[320]{0:T(512)} %param.32) | copy-start | bytes 3844
  191.9 71.5 %copy-start.3 = (bf16[64,2560]{1,0:T(8,128)(2,1)S(1)}, bf16[64,2560]{1,0:T(8,128)(2,1)}, u32[]{:S(2)}) copy-start(bf16[64,2560]{1,0:T(8,128)(2,1)} %param.21) | copy-start | bytes 983044
  191.9 72.7 %copy-start.8 = (f32[2560]{0:T(1024)S(1)}, f32[2560]{0:T(1024)}, u32[]{:S(2)}) copy-start(f32[2560]{0:T(1024)} %param.34) | copy-start | bytes 30724
  191.9 116.4 %all-gather.8.cloned.1.call-start = ((), (), s32[]{:S(2)}) async-start(), calls=%async_computation.4 | async-start | bytes 5570560 | tf_op jit(solution)/shard_map/all_gather | solution.py:149
  266.4 121.2 %reduce-scatter.5.cloned.1.call-start = ((), (), s32[]{:S(2)}) async-start(), calls=%async_computation.5 | async-start | bytes 5570560 | tf_op jit(solution)/shard_map/reduce_scatter | solution.py:154
  323.6 64.0 %copy-start.4 = (bf16[64,2560]{1,0:T(8,128)(2,1)S(1)}, bf16[64,2560]{1,0:T(8,128)(2,1)}, u32[]{:S(2)}) copy-start(bf16[64,2560]{1,0:T(8,128)(2,1)} %reduce-scatter.3.cloned.1.call-done) | copy-start | bytes 983044
  (2 other events, 2.6 us)
Sparse Core Ops, SparseCore 0:
  9.2 46.0 all-gather.5
  100.2 43.6 all-gather.9
  192.1 71.2 reduce-scatter.2
  266.5 41.7 all-gather.7
  323.7 63.8 reduce-scatter.4
where the time goes:
time: 397 us; the launch traced here: 396 us
  waiting for transfers between devices  230 us (58%)
  blocking collectives  55.3 us (14%)
  matrix products  47.1 us (12%)
  other arithmetic  31.4 us (8%)
  between operations  14.2 us (4%)
  local copies, waits for them, and re-layouts  10.9 us (3%)
  starting transfers between devices  7.17 us (2%)
    reduce_scatter x1, waiting for transfers between devices, local(): lax.psum_scatter(jnp.dot(piece, w_out, preferred_element_type=jnp.float32...  71.4 us
    reduce_scatter x1, waiting for transfers between devices, local(): lax.psum_scatter(jnp.dot(piece, w_down, preferred_element_type=jnp.float3...  64 us
    all_gather x1, waiting for transfers between devices, local(): gathered = lax.all_gather(tokens, 'tp', axis=0, tiled=True)  45.6 us
    all_gather x1, waiting for transfers between devices, local(): mlp_in = lax.all_gather(normed_own, 'tp', axis=0, tiled=True)  41.6 us
    unnamed x1, blocking collectives  31.3 us
    psum x1, blocking collectives, local(): squares = lax.psum(jnp.sum(gated * gated, axis=-1), 'tp')  23.9 us
    dot_general x1, matrix products, local(): jnp.dot(piece, w_down, preferred_element_type=jnp.float32)  10.4 us
    dot_general x1, matrix products, local(): jnp.einsum('btsh,bshp->bthp', mixed_w, scaled, precision=lax.Precision.HI...  8.52 us
  transfers between devices with their start and end apart: 7, of which 6 were waited for; matrix products, arithmetic and copies ran while one was open for 4% of the time, Pallas kernels for 0%

commit v1 on v0

--- a/solution.py
+++ b/solution.py
@@ -81,7 +81,9 @@
     w_up,
     w_down,
 ):
-    gathered = lax.all_gather(tokens, "tp", axis=0, tiled=True)
+    gathered = jnp.concatenate(
+        lax.all_to_all(jnp.stack([tokens] * lax.axis_size("tp")), "tp", 0, 0), axis=0
+    )
     normed = rms_rows(gathered, norm1_gain).astype(jnp.bfloat16)
     bc_rows = jnp.dot(normed, w_bc, preferred_element_type=jnp.float32).astype(jnp.bfloat16)
     group_len = gathered.shape[0]

time: 397 us -> 481 us (1.21)
  waiting for transfers between devices: 230 us -> 300 us
  starting transfers between devices: 7.17 us -> 16.1 us
    all_to_all x0 -> x1, waiting for transfers between devices: none -> 117 us  [local(): lax.all_to_all(jnp.stack([tokens] * lax.axis_size('tp')), 'tp', 0, 0)]
    all_gather x1 -> x0, waiting for transfers between devices: 45.6 us -> none  [local(): gathered = lax.all_gather(tokens, 'tp', axis=0, tiled=True)]
    all_to_all x0 -> x1, starting transfers between devices: none -> 8.75 us  [local(): lax.all_to_all(jnp.stack([tokens] * lax.axis_size('tp')), 'tp', 0, 0)]
  transfers between devices with their start and end apart: 7 -> 7, of which waited for: 6 -> 6; matrix products, arithmetic and copies ran while one was open for 4% -> 3% of each run, Pallas kernels for 0% -> 0%
where the time goes in v1:
time: 481 us; the launch traced here: 479 us
  waiting for transfers between devices  300 us (62%)
  blocking collectives  55.2 us (11%)
  matrix products  47.1 us (10%)
  other arithmetic  33.7 us (7%)
  starting transfers between devices  16.1 us (3%)
  between operations  14.3 us (3%)
  local copies, waits for them, and re-layouts  12.3 us (3%)
    all_to_all x1, waiting for transfers between devices, local(): lax.all_to_all(jnp.stack([tokens] * lax.axis_size('tp')), 'tp', 0, 0)  117 us
    reduce_scatter x1, waiting for transfers between devices, local(): lax.psum_scatter(jnp.dot(piece, w_out, preferred_element_type=jnp.float32...  71.4 us
    reduce_scatter x1, waiting for transfers between devices, local(): lax.psum_scatter(jnp.dot(piece, w_down, preferred_element_type=jnp.float3...  64 us
    all_gather x1, waiting for transfers between devices, local(): mlp_in = lax.all_gather(normed_own, 'tp', axis=0, tiled=True)  41.6 us
    unnamed x1, blocking collectives  31.3 us
    psum x1, blocking collectives, local(): squares = lax.psum(jnp.sum(gated * gated, axis=-1), 'tp')  24 us
    dot_general x1, matrix products, local(): jnp.dot(piece, w_down, preferred_element_type=jnp.float32)  10.4 us
  transfers between devices with their start and end apart: 7, of which 6 were waited for; matrix products, arithmetic and copies ran while one was open for 3% of the time, Pallas kernels for 0%

profile of v1, /device:TPU:4, one launch (start us, length us, event | category | flops | bytes accessed | tf_op | source)
XLA Modules:
  0.0 479.3 jit_solution(4969441931090197968)
XLA Ops:
  6.5 3.9 stack.2
  10.5 8.7 %all-to-all-start = ((bf16[16,64,2560]{2,1,0:T(8,128)(2,1)}), bf16[16,64,2560]{2,1,0:T(8,128)(2,1)}, u32[]{:S(2)}, u32[]{:S(2)}) async-start(bf16[16,64,2560]{2,1,0:T(8,128)(2,1)} %stack.2), calls=%async_computation | async-start | bytes 10485760 | tf_op jit(solution)/shard_map/all_to_all | solution.py:85
  19.4 116.6 %all-to-all-done = bf16[16,64,2560]{2,1,0:T(8,128)(2,1)} async-done(((bf16[16,64,2560]{2,1,0:T(8,128)(2,1)}), bf16[16,64,2560]{2,1,0:T(8,128)(2,1)}, u32[]{:S(2)}, u32[]{:S(2)}) %all-to-all-start) | async-done | bytes 5242912 | tf_op jit(solution)/shard_map/all_to_all | solution.py:85
  136.0 3.6 multiply_reduce_fusion
  139.7 3.8 fusion.2
  145.8 6.0 %reduce-window.6 = f32[4,5,2,128]{3,2,1,0:T(2,128)S(1)} reduce-window(f32[4,5,2,128]{3,2,1,0:T(2,128)S(1)} %copy.60, f32[]{:T(128)} %constant.61.clone.1), window={size=1x1x1x128 pad=0_0x0_0x0_0x127_0}, to_apply=%region_1.2 | reduce-window | flops 650240 | bytes 40964 | tf_op jit(solution)/shard_map/reduce-window
  152.8 4.5 convolution_convert_fusion.3
  157.4 3.5 collective-permute-start.1
  162.9 3.5 collective-permute-start
  167.3 4.1 collective-permute-done
  174.1 2.8 reshape.122
  179.1 3.2 while.26
  184.7 31.3 %all-reduce = bf16[80]{0:T(256)(128)(2,1)S(1)} all-reduce(bf16[80]{0:T(256)(128)(2,1)S(1)} %dynamic-update-slice), channel_id=3, replica_groups=mesh['ctx'=16,'tp'=16] {'ctx'}, use_global_device_ids=true, to_apply=%add | all-reduce | flops 80 | bytes 320
  216.3 8.5 %fusion.16 = f32[4,256,5,64]{1,3,2,0:T(8,128)} fusion(f32[4,256,5]{1,2,0:T(8,128)S(1)} %copy.64, f32[4,256,256]{2,1,0:T(8,128)S(1)} %fusion.49, pred[256,256]{1,0:T(8,128)(4,1)S(1)} %iota_compare_fusion, f32[4,256,5,64]{1,0,3,2:T(4,128)} %reshape.122, f32[4,256,5]{1,2,0:T(8,128)S(1)} %bitcast.104), kind=kOutput, calls=%fused_computation.27 | convolution fusion | flops 1012203520 | bytes 3776512 | tf_op jit(solution)/shard_map/btsh,bshp->bthp/dot_general | solution.py:115
  227.3 8.3 %while.25 = (s32[]{:T(128)}, f32[5,64,128]{2,1,0:T(8,128)S(1)}, s32[]{:T(128)}, bf16[16,5,64,128]{3,2,1,0:T(8,128)(2,1)}, bf16[16,5]{1,0:T(8,128)(2,1)S(1)}, /*index=5*/s32[]{:T(128)}, s32[]{:T(128)}, s32[]{:T(128)}) while((s32[]{:T(128)}, f32[5,64,128]{2,1,0:T(8,128)S(1)}, s32[]{:T(128)}, bf16[16,5,64,128]{3,2,1,0:T(8,128)(2,1)}, ...), condition=%wide.region_8.9_spmd, body=%wide.region_7.8_spmd.sunk | while | flops 122890 | bytes 409785 | solution.py:36
  235.6 3.0 fusion.15
  241.4 3.1 multiply_reduce_fusion.1
  244.5 24.0 %psum.7 = f32[1024]{0:T(1024)S(1)} all-reduce(f32[1024]{0:T(1024)S(1)} %get-tuple-element.135), channel_id=1, replica_groups=mesh['ctx'=16,'tp'=16] {'tp'}, use_global_device_ids=true, to_apply=%region_10.11 | all-reduce | flops 1024 | bytes 8192 | tf_op jit(solution)/shard_map/psum | solution.py:138
  268.5 6.8 %convolution_convert_fusion.1 = bf16[1024,2560]{1,0:T(8,128)(2,1)} fusion(bf16[320,2560]{1,0:T(8,128)(2,1)S(1)} %copy-done, f32[320]{0:T(512)S(1)} %copy-done.14, f32[1024]{0:T(1024)S(1)} %add_rsqrt_fusion.1, f32[1024,320]{0,1:T(8,128)} %bitcast.100, f32[1024,320]{0,1:T(8,128)} %get-tuple-element.136), kind=kOutput, calls=%fused_computation.11 | convolution fusion | flops 1682964480 | bytes 9508096 | tf_op jit(solution)/shard_map/dot_general | solution.py:144
  275.4 71.4 %reduce-scatter.3.cloned.1.call-done = bf16[64,2560]{1,0:T(8,128)(2,1)} async-done(((bf16[1024,2560]{1,0:T(8,128)(2,1)}), bf16[64,2560]{1,0:T(8,128)(2,1)}) %reduce-scatter.3.cloned.1.call-update) | async-done | bytes 327696 | tf_op jit(solution)/shard_map/reduce_scatter | solution.py:143
  350.1 41.6 %all-gather.5.cloned.1.call-done = bf16[1024,2560]{1,0:T(8,128)(2,1)} async-done(((bf16[64,2560]{1,0:T(8,128)(2,1)}), bf16[1024,2560]{1,0:T(8,128)(2,1)}) %all-gather.5.cloned.1.call-update) | async-done | bytes 5242896 | tf_op jit(solution)/shard_map/all_gather | solution.py:151
  391.7 4.9 %fusion.50 = f32[1024,320]{0,1:T(8,128)S(1)} fusion(bf16[1024,2560]{1,0:T(8,128)(2,1)} %all-gather.5.cloned.1.call-done, bf16[2560,320]{0,1:T(8,128)(2,1)} %param.35), kind=kOutput, calls=%fused_computation.97 | convolution fusion | flops 1677721600 | bytes 8192000 | tf_op jit(solution)/shard_map/dot_general | solution.py:152
  396.6 10.4 %convolution_convert_fusion = bf16[1024,2560]{1,0:T(8,128)(2,1)} fusion(bf16[320,2560]{1,0:T(8,128)(2,1)} %param.37, bf16[1024,2560]{1,0:T(8,128)(2,1)} %all-gather.5.cloned.1.call-done, bf16[2560,320]{0,1:T(8,128)(2,1)} %param.36, f32[1024,320]{0,1:T(8,128)S(1)} %fusion.50), kind=kOutput, calls=%fused_computation.10 | convolution fusion | flops 3360030720 | bytes 15073280 | tf_op jit(solution)/shard_map/dot_general | solution.py:157
  407.0 64.0 %reduce-scatter.5.cloned.1.call-done = bf16[64,2560]{1,0:T(8,128)(2,1)} async-done(((bf16[1024,2560]{1,0:T(8,128)(2,1)}), bf16[64,2560]{1,0:T(8,128)(2,1)}) %reduce-scatter.5.cloned.1.call-update) | async-done | bytes 327696 | tf_op jit(solution)/shard_map/reduce_scatter | solution.py:156
  (134 shorter events, 34.6 us)
Async XLA Ops:
  6.5 262.0 %copy-start = (bf16[320,2560]{1,0:T(8,128)(2,1)S(1)}, bf16[320,2560]{1,0:T(8,128)(2,1)}, u32[]{:S(2)}) copy-start(bf16[320,2560]{1,0:T(8,128)(2,1)} %param.33) | copy-start | bytes 4915204
  10.5 8.8 %copy-start.15 = (f32[5]{0:T(128)S(1)}, f32[5]{0:T(128)}, u32[]{:S(2)}) copy-start(f32[5]{0:T(128)} %param.28) | copy-start | bytes 64
  10.5 8.8 %copy-start.8 = (f32[4,320]{1,0:T(4,128)S(1)}, f32[4,320]{1,0:T(4,128)}, u32[]{:S(2)}) copy-start(f32[4,320]{1,0:T(4,128)} %param.29) | copy-start | bytes 15364
  10.5 8.9 %copy-start.9 = (f32[4,256]{1,0:T(4,128)S(1)}, f32[4,256]{1,0:T(4,128)}, u32[]{:S(2)}) copy-start(f32[4,256]{1,0:T(4,128)} %param.30) | copy-start | bytes 12292
  10.5 125.6 %all-to-all-start = ((bf16[16,64,2560]{2,1,0:T(8,128)(2,1)}), bf16[16,64,2560]{2,1,0:T(8,128)(2,1)}, u32[]{:S(2)}, u32[]{:S(2)}) async-start(bf16[16,64,2560]{2,1,0:T(8,128)(2,1)} %stack.2), calls=%async_computation | async-start | bytes 10485760 | tf_op jit(solution)/shard_map/all_to_all | solution.py:85
  19.2 208.1 %all-gather.7.cloned.1.call-start = ((), (), s32[]{:S(2)}) async-start(), calls=%async_computation.6 | async-start | bytes 1392640 | tf_op jit(solution)/shard_map/all_gather | solution.py:22
  19.4 120.3 %copy-start.6 = (f32[2560]{0:T(1024)S(1)}, f32[2560]{0:T(1024)}, u32[]{:S(2)}) copy-start(f32[2560]{0:T(1024)} %param.22) | copy-start | bytes 30724
  152.4 8.5 %slice-start = ((s8[5242880]{0:T(1024)(128)(4,1)}), s8[1048576]{0:T(1024)(128)(4,1)S(1)}, s32[]{:S(2)}) async-start(s8[5242880]{0:T(1024)(128)(4,1)} %bitcast.90), calls=%async_computation.7 | async-start | bytes 2097152
  152.8 8.1 %slice-start.1 = ((s8[5242880]{0:T(1024)(128)(4,1)}), s8[4194304]{0:T(1024)(128)(4,1)S(1)}, s32[]{:S(2)}) async-start(s8[5242880]{0:T(1024)(128)(4,1)} %bitcast.90), calls=%async_computation.8 | async-start | bytes 8388608
  152.8 8.1 %copy-start.12 = (bf16[2560,320]{0,1:T(8,128)(2,1)S(1)}, bf16[2560,320]{0,1:T(8,128)(2,1)}, u32[]{:S(2)}) copy-start(bf16[2560,320]{0,1:T(8,128)(2,1)} %param.24) | copy-start | bytes 4915204
  157.4 9.1 %collective-permute-start.1 = (bf16[3,256]{1,0:T(4,128)(2,1)S(1)}, bf16[3,256]{1,0:T(4,128)(2,1)S(1)}, u32[]{:S(2)}, u32[]{:S(2)}) collective-permute-start(bf16[3,256]{1,0:T(4,128)(2,1)S(1)} %slice.97), channel_id=1, source_target_pairs={{0,16},{16,32},{32,48},{48,64},{64,80},{80,96},{96,112},{112,128},... | collective-permute-start | bytes 4616 | tf_op jit(solution)/shard_map/ppermute | solution.py:16
  162.9 8.4 %collective-permute-start = (bf16[3,320]{0,1:T(8,128)(2,1)S(1)}, bf16[3,320]{0,1:T(8,128)(2,1)S(1)}, u32[]{:S(2)}, u32[]{:S(2)}) collective-permute-start(bf16[3,320]{0,1:T(8,128)(2,1)S(1)} %slice.92), channel_id=1, source_target_pairs={{0,16},{16,32},{32,48},{48,64},{64,80},{80,96},{96,112},{112,128},... | collective-permute-start | bytes 5768 | tf_op jit(solution)/shard_map/ppermute | solution.py:16
  179.1 4.0 copy-start.16
  183.0 163.8 %reduce-scatter.3.cloned.1.call-start = ((), (), s32[]{:S(2)}) async-start(), calls=%async_computation.3 | async-start | bytes 5570560 | tf_op jit(solution)/shard_map/reduce_scatter | solution.py:143
  224.9 10.8 %copy-start.11 = (f32[5]{0:T(128)S(1)}, f32[5]{0:T(128)}, u32[]{:S(2)}) copy-start(f32[5]{0:T(128)} %param.31) | copy-start | bytes 64
  227.3 12.5 %slice-start.2 = ((s8[5242880]{0:T(1024)(128)(4,1)}), s8[1048576]{0:T(1024)(128)(4,1)S(1)}, s32[]{:S(2)}) async-start(s8[5242880]{0:T(1024)(128)(4,1)} %bitcast.92), calls=%async_computation.9 | async-start | bytes 2097152
  235.6 4.2 slice-start.3
  239.8 4.7 copy-start.4
  241.4 27.1 %copy-start.14 = (f32[320]{0:T(512)S(1)}, f32[320]{0:T(512)}, u32[]{:S(2)}) copy-start(f32[320]{0:T(512)} %param.32) | copy-start | bytes 3844
  275.3 71.4 %copy-start.2 = (bf16[64,2560]{1,0:T(8,128)(2,1)S(1)}, bf16[64,2560]{1,0:T(8,128)(2,1)}, u32[]{:S(2)}) copy-start(bf16[64,2560]{1,0:T(8,128)(2,1)} %param.21) | copy-start | bytes 983044
  275.3 72.6 %copy-start.7 = (f32[2560]{0:T(1024)S(1)}, f32[2560]{0:T(1024)}, u32[]{:S(2)}) copy-start(f32[2560]{0:T(1024)} %param.34) | copy-start | bytes 30724
  275.3 116.3 %all-gather.5.cloned.1.call-start = ((), (), s32[]{:S(2)}) async-start(), calls=%async_computation.4 | async-start | bytes 5570560 | tf_op jit(solution)/shard_map/all_gather | solution.py:151
  349.8 121.2 %reduce-scatter.5.cloned.1.call-start = ((), (), s32[]{:S(2)}) async-start(), calls=%async_computation.5 | async-start | bytes 5570560 | tf_op jit(solution)/shard_map/reduce_scatter | solution.py:156
  407.0 64.0 %copy-start.3 = (bf16[64,2560]{1,0:T(8,128)(2,1)S(1)}, bf16[64,2560]{1,0:T(8,128)(2,1)}, u32[]{:S(2)}) copy-start(bf16[64,2560]{1,0:T(8,128)(2,1)} %reduce-scatter.3.cloned.1.call-done) | copy-start | bytes 983044
  (4 other events, 11.7 us)
Sparse Core Ops, SparseCore 0:
  183.1 44.1 all-gather.6
  275.5 71.2 reduce-scatter.2
  349.9 41.7 all-gather.4
  407.1 63.8 reduce-scatter.4
